TPU v7x, 32 devices: a whole 2x2x4 slice. The times are simulated.
32 devices in a mesh: grp: 4 (over x, core), ep: 8 (over z, y).
Axes of the slice: x: 2, y: 2, z: 4, core: 2. Of those that a mesh axis runs over, the one named last changes fastest.
Arguments:
- tokens: bfloat16 [2048, 5120], P('ep', 'grp'), may hold values from -6 to 6
- cotangent: bfloat16 [2048, 5120], P('ep', 'grp'), may hold values from -0.59765625 to 0.59765625
- gate_weights: bfloat16 [2048, 6], P('ep'), may hold values from 0.099609375 to 1
- expert_ids: int32 [2048, 6], P('ep'), may hold values from 0 to 159, all different within a row; in each aligned block of 256 rows (0 to 255, 256 to 511, ...) at most 16 rows name the same one
- hot_ids: int32 [2], replicated, may hold values from 8 to 159, as said below
- gate_cold: bfloat16 [8, 5120, 768], P('ep', 'grp'), may hold values from -0.078125 to 0.078125
- up_cold: bfloat16 [8, 5120, 768], P('ep', 'grp'), may hold values from -0.078125 to 0.078125
- down_cold: bfloat16 [8, 768, 5120], P('ep', None, 'grp'), may hold values from -0.21875 to 0.21875
- gate_hot: bfloat16 [2, 5120, 768], P(None, 'grp', 'ep'), may hold values from -0.078125 to 0.078125
- up_hot: bfloat16 [2, 5120, 768], P(None, 'grp', 'ep'), may hold values from -0.078125 to 0.078125
- down_hot: bfloat16 [2, 768, 5120], P(None, 'ep', 'grp'), may hold values from -0.21875 to 0.21875
Outputs:
- grad_gate_cold: bfloat16 [8, 5120, 768], P('ep', 'grp')
- grad_up_cold: bfloat16 [8, 5120, 768], P('ep', 'grp')
- grad_down_cold: bfloat16 [8, 768, 5120], P('ep', None, 'grp')
- grad_gate_hot: float32 [2, 5120, 768], P(None, 'grp', 'ep')
- grad_up_hot: float32 [2, 5120, 768], P(None, 'grp', 'ep')
- grad_down_hot: float32 [2, 768, 5120], P(None, 'ep', 'grp')
- gate_weight_grad: float32 [2048, 6], P('ep')
Inputs may be any that keep to these rules, and one draw needn't show every extreme that they name: `expert_ids`: each row names 6 different experts. Among the routes of the 256 tokens of one index of ep (aligned blocks of rows) no expert is named more than 16 times, a bound that some block reaches. `hot_ids`: distinct expert numbers, none below 8; expert 160 - 1 is always among them.
All inputs are finite; a program needn't handle non-finite values.
Results may differ from a plain program's by a relative error of at most 0.02.
Values may be sent and summed in bfloat16 or wider, within the bound.
No kernel may reach another device: no remote copies, remote signals or barrier semaphores. Data moves between devices by JAX's collectives and lax.ppermute only.
A program may use at most 128 MiB of HBM per device.

v0:
```python
import jax
import jax.numpy as jnp
from jax import lax
from jax.sharding import PartitionSpec as P


def route_table(flat_ids, targets, capacity):
    matches = (flat_ids[:, None] == targets[None, :]).astype(jnp.int32)
    rank_of = jnp.cumsum(matches, axis=0) - 1
    slot_of = jnp.sum(matches * rank_of, axis=1)
    owner_of = jnp.sum(matches * jnp.arange(targets.shape[0], dtype=jnp.int32)[None, :], axis=1)
    usable = jnp.sum(matches, axis=1) > 0
    row_of = owner_of * capacity + slot_of
    rows_total = targets.shape[0] * capacity
    route_map = (row_of[None, :] == jnp.arange(rows_total, dtype=jnp.int32)[:, None]) & usable[
        None, :
    ]
    return route_map.astype(jnp.float32)


def gather_rows(route_map, tokens, cotangent, flat_weights, tok_rows, top_count):
    per_token = jnp.sum(route_map.reshape(route_map.shape[0], tok_rows, top_count), axis=2)
    token_map = per_token.astype(jnp.bfloat16)
    feat_rows = jnp.dot(token_map, tokens, preferred_element_type=jnp.float32).astype(jnp.bfloat16)
    cotan_rows = jnp.dot(token_map, cotangent, preferred_element_type=jnp.float32).astype(
        jnp.bfloat16
    )
    scale_rows = jnp.dot(
        route_map, flat_weights.astype(jnp.float32), precision=lax.Precision.HIGHEST
    )
    return (feat_rows, cotan_rows, scale_rows.astype(jnp.bfloat16))


def swiglu_back(pre_gate, pre_up, grad_hidden):
    sigmoid_gate = jax.nn.sigmoid(pre_gate)
    activated = pre_gate * sigmoid_gate
    hidden = (activated * pre_up).astype(jnp.bfloat16)
    back_gate = (
        grad_hidden * pre_up * sigmoid_gate * (1.0 + pre_gate * (1.0 - sigmoid_gate))
    ).astype(jnp.bfloat16)
    back_up = (grad_hidden * activated).astype(jnp.bfloat16)
    return (hidden, back_gate, back_up)


def body(
    tokens,
    cotangent,
    gate_weights,
    expert_ids,
    hot_ids,
    gate_cold,
    up_cold,
    down_cold,
    gate_hot,
    up_hot,
    down_hot,
):
    tok_rows, slice_width = tokens.shape
    top_count = expert_ids.shape[1]
    cold_count = lax.axis_size("ep")
    hot_count = hot_ids.shape[0]
    capacity = tok_rows // 16
    flat_ids = expert_ids.reshape(-1)
    flat_weights = gate_weights.reshape(-1)
    cold_map = route_table(flat_ids, jnp.arange(cold_count, dtype=jnp.int32), capacity)
    hot_map = route_table(flat_ids, hot_ids, capacity)
    cold_feats, cold_cotan, cold_scale = gather_rows(
        cold_map, tokens, cotangent, flat_weights, tok_rows, top_count
    )
    hot_feats, hot_cotan, hot_scale = gather_rows(
        hot_map, tokens, cotangent, flat_weights, tok_rows, top_count
    )
    outgoing = (
        cold_feats.reshape(cold_count, capacity, slice_width),
        cold_cotan.reshape(cold_count, capacity, slice_width),
        cold_scale.reshape(cold_count, capacity),
    )
    recv_feats, recv_cotan, recv_scale = (
        lax.all_to_all(outgoing[0], "ep", split_axis=0, concat_axis=0, tiled=True),
        lax.all_to_all(outgoing[1], "ep", split_axis=0, concat_axis=0, tiled=True),
        lax.all_to_all(outgoing[2], "ep", split_axis=0, concat_axis=0, tiled=True),
    )
    recv_feats = recv_feats.reshape(-1, slice_width)
    recv_cotan = recv_cotan.reshape(-1, slice_width)
    weighted = (
        recv_scale.reshape(-1).astype(jnp.float32)[:, None] * recv_cotan.astype(jnp.float32)
    ).astype(jnp.bfloat16)
    w_gate = gate_cold[0]
    w_up = up_cold[0]
    w_down = down_cold[0]
    part_gate = jnp.dot(recv_feats, w_gate, preferred_element_type=jnp.float32)
    part_up = jnp.dot(recv_feats, w_up, preferred_element_type=jnp.float32)
    part_hidden = lax.dot_general(
        weighted, w_down, (((1,), (1,)), ((), ())), preferred_element_type=jnp.float32
    )
    pre_gate, pre_up, grad_hidden = (
        lax.psum(part_gate.astype(jnp.bfloat16), "grp").astype(jnp.float32),
        lax.psum(part_up.astype(jnp.bfloat16), "grp").astype(jnp.float32),
        lax.psum(part_hidden.astype(jnp.bfloat16), "grp").astype(jnp.float32),
    )
    hidden, back_gate, back_up = swiglu_back(pre_gate, pre_up, grad_hidden)
    output_slice = jnp.dot(hidden, w_down, preferred_element_type=jnp.float32)
    cold_route = jnp.sum(output_slice * recv_cotan.astype(jnp.float32), axis=1)
    contract_rows = (((0,), (0,)), ((), ()))
    grad_gate_cold = lax.dot_general(
        recv_feats, back_gate, contract_rows, preferred_element_type=jnp.float32
    )
    grad_up_cold = lax.dot_general(
        recv_feats, back_up, contract_rows, preferred_element_type=jnp.float32
    )
    grad_down_cold = lax.dot_general(
        hidden, weighted, contract_rows, preferred_element_type=jnp.float32
    )
    hot_feats = hot_feats.reshape(hot_count, capacity, slice_width)
    hot_cotan = hot_cotan.reshape(hot_count, capacity, slice_width)
    hot_scale = hot_scale.reshape(hot_count, capacity)
    full_gate, full_up = (
        lax.all_gather(gate_hot, "ep", axis=2, tiled=True),
        lax.all_gather(up_hot, "ep", axis=2, tiled=True),
    )
    full_down = lax.all_gather(down_hot, "ep", axis=1, tiled=True)
    hot_weighted = (
        hot_scale.astype(jnp.float32)[:, :, None] * hot_cotan.astype(jnp.float32)
    ).astype(jnp.bfloat16)
    part_gate_hot = jnp.einsum(
        "jcd,jdh->jch", hot_feats, full_gate, preferred_element_type=jnp.float32
    )
    part_up_hot = jnp.einsum("jcd,jdh->jch", hot_feats, full_up, preferred_element_type=jnp.float32)
    part_hidden_hot = jnp.einsum(
        "jcd,jhd->jch", hot_weighted, full_down, preferred_element_type=jnp.float32
    )
    pre_gate_hot, pre_up_hot, grad_hidden_hot = (
        lax.psum(part_gate_hot.astype(jnp.bfloat16), "grp").astype(jnp.float32),
        lax.psum(part_up_hot.astype(jnp.bfloat16), "grp").astype(jnp.float32),
        lax.psum(part_hidden_hot.astype(jnp.bfloat16), "grp").astype(jnp.float32),
    )
    hidden_hot, back_gate_hot, back_up_hot = swiglu_back(pre_gate_hot, pre_up_hot, grad_hidden_hot)
    output_hot = jnp.einsum(
        "jch,jhd->jcd", hidden_hot, full_down, preferred_element_type=jnp.float32
    )
    hot_route_part = jnp.sum(output_hot * hot_cotan.astype(jnp.float32), axis=2)
    shadow_gate = jnp.einsum(
        "jcd,jch->jdh", hot_feats, back_gate_hot, preferred_element_type=jnp.float32
    )
    shadow_up = jnp.einsum(
        "jcd,jch->jdh", hot_feats, back_up_hot, preferred_element_type=jnp.float32
    )
    shadow_down = jnp.einsum(
        "jch,jcd->jdh", hidden_hot, hot_weighted, preferred_element_type=jnp.float32
    )
    grad_gate_hot, grad_up_hot, down_turned = (
        lax.psum_scatter(
            shadow_gate.astype(jnp.bfloat16), "ep", scatter_dimension=2, tiled=True
        ).astype(jnp.float32),
        lax.psum_scatter(
            shadow_up.astype(jnp.bfloat16), "ep", scatter_dimension=2, tiled=True
        ).astype(jnp.float32),
        lax.psum_scatter(
            shadow_down.astype(jnp.bfloat16), "ep", scatter_dimension=2, tiled=True
        ).astype(jnp.float32),
    )
    grad_down_hot = jnp.transpose(down_turned, (0, 2, 1))
    cold_route, hot_route = lax.psum((cold_route, hot_route_part), "grp")
    cold_back = lax.all_to_all(
        cold_route.reshape(cold_count, capacity), "ep", split_axis=0, concat_axis=0, tiled=True
    )
    route_flat = jnp.dot(cold_back.reshape(-1), cold_map, precision=lax.Precision.HIGHEST)
    route_flat = route_flat + jnp.dot(
        hot_route.reshape(-1), hot_map, precision=lax.Precision.HIGHEST
    )
    gate_weight_grad = route_flat.reshape(tok_rows, top_count)
    return (
        grad_gate_cold[None].astype(jnp.bfloat16),
        grad_up_cold[None].astype(jnp.bfloat16),
        grad_down_cold[None].astype(jnp.bfloat16),
        grad_gate_hot,
        grad_up_hot,
        grad_down_hot,
        gate_weight_grad,
    )


def solution(mesh):
    in_specs = (
        P("ep", "grp"),
        P("ep", "grp"),
        P("ep", None),
        P("ep", None),
        P(),
        P("ep", "grp", None),
        P("ep", "grp", None),
        P("ep", None, "grp"),
        P(None, "grp", "ep"),
        P(None, "grp", "ep"),
        P(None, "ep", "grp"),
    )
    out_specs = (
        P("ep", "grp", None),
        P("ep", "grp", None),
        P("ep", None, "grp"),
        P(None, "grp", "ep"),
        P(None, "grp", "ep"),
        P(None, "ep", "grp"),
        P("ep", None),
    )
    return jax.shard_map(body, mesh=mesh, in_specs=in_specs, out_specs=out_specs, check_vma=False)
```

profile of v0, /device:TPU:0, one launch (start us, length us, event | category | flops | bytes accessed | tf_op | source)
XLA Modules:
  0.0 574.7 jit_solution(6589414462695450256)
XLA Ops:
  7.2 0.7 all-gather.8.cloned.1.call-update
  8.0 0.7 all-gather.6.cloned.1.call-update
  8.7 0.7 all-gather.4.cloned.1.call-update
  9.4 1.5 copy.29
  10.9 1.0 eq.93
  12.0 1.0 eq.88
  13.0 0.8 copy.33
  14.0 2.3 reduce-window.14
  16.3 0.3 slice_reduce_fusion
  16.9 0.3 fusion.23
  17.2 0.7 all_to_all.24
  17.9 7.3 %all-to-all-start.1 = ((bf16[8,1,16]{2,1,0:T(2,128)(2,1)}), bf16[8,1,16]{2,1,0:T(2,128)(2,1)S(1)}, u32[]{:S(2)}, u32[]{:S(2)}) async-start(bf16[8,1,16]{2,1,0:T(2,128)(2,1)} %all_to_all.24), calls=%async_computation.1 | async-start | bytes 8192 | tf_op jit(solution)/shard_map/all_to_all | solution.py:81
  25.2 0.8 add.66
  26.1 0.7 compare_convert_fusion.1
  26.9 0.6 reduce-window.16
  27.4 0.2 slice_reduce_fusion.1
  27.6 0.2 reduce-window.19
  27.9 0.8 fusion.77
  28.7 0.8 add.70
  29.5 1.0 copy.36
  30.5 0.2 gt.25
  30.7 1.0 copy.31
  32.0 0.2 convolution_convert_fusion.9
  32.3 1.0 convolution_convert_fusion.7
  33.3 0.2 convolution_convert_fusion.8
  33.5 6.0 %all-to-all-start = ((bf16[8,16,1280]{2,1,0:T(8,128)(2,1)}), bf16[8,16,1280]{2,1,0:T(8,128)(2,1)S(1)}, u32[]{:S(2)}, u32[]{:S(2)}) async-start(bf16[8,16,1280]{2,1,0:T(8,128)(2,1)} %bitcast.121), calls=%async_computation | async-start | bytes 655360 | tf_op jit(solution)/shard_map/all_to_all | solution.py:79
  39.8 1.0 convolution_convert_fusion.6
  40.7 11.0 %all-to-all-done = bf16[8,16,1280]{2,1,0:T(8,128)(2,1)S(1)} async-done(((bf16[8,16,1280]{2,1,0:T(8,128)(2,1)}), bf16[8,16,1280]{2,1,0:T(8,128)(2,1)S(1)}, u32[]{:S(2)}, u32[]{:S(2)}) %all-to-all-start) | async-done | bytes 327712 | tf_op jit(solution)/shard_map/all_to_all | solution.py:79
  51.8 5.0 all-to-all-start.2
  56.8 2.7 fusion.16
  59.4 2.7 fusion.19
  62.1 13.3 %all-to-all-done.2 = bf16[8,16,1280]{2,1,0:T(8,128)(2,1)S(1)} async-done(((bf16[8,16,1280]{2,1,0:T(8,128)(2,1)}), bf16[8,16,1280]{2,1,0:T(8,128)(2,1)S(1)}, u32[]{:S(2)}, u32[]{:S(2)}) %all-to-all-start.2) | async-done | bytes 327712 | tf_op jit(solution)/shard_map/all_to_all | solution.py:80
  75.5 12.9 %all-gather.8.cloned.1.call-done = bf16[2,1280,768]{1,2,0:T(8,128)(2,1)} async-done(((bf16[2,1280,96]{1,2,0:T(8,128)(2,1)}), bf16[2,1280,768]{1,2,0:T(8,128)(2,1)}) %all-gather.8.cloned.1.call-update) | async-done | bytes 3932176 | tf_op jit(solution)/shard_map/all_gather | solution.py:118
  88.4 3.9 convolution_convert_fusion.10
  92.3 67.5 %all-gather.6.cloned.1.call-done = bf16[2,1280,768]{1,2,0:T(8,128)(2,1)} async-done(((bf16[2,1280,96]{1,2,0:T(8,128)(2,1)}), bf16[2,1280,768]{1,2,0:T(8,128)(2,1)}) %all-gather.6.cloned.1.call-update) | async-done | bytes 3932176 | tf_op jit(solution)/shard_map/all_gather | solution.py:119
  159.7 3.9 convolution_convert_fusion.11
  163.6 66.8 %all-gather.4.cloned.1.call-done = bf16[2,768,1280]{2,1,0:T(8,128)(2,1)} async-done(((bf16[2,96,1280]{2,1,0:T(8,128)(2,1)}), bf16[2,768,1280]{2,1,0:T(8,128)(2,1)}) %all-gather.4.cloned.1.call-update) | async-done | bytes 3932176 | tf_op jit(solution)/shard_map/all_gather | solution.py:121
  230.4 3.9 convolution_convert_fusion.12
  234.4 1.5 fusion.13
  235.9 27.8 %all-reduce.6.cloned.1.call-done = (bf16[2,16,768]{2,1,0:T(8,128)(2,1)}, bf16[2,16,768]{2,1,0:T(8,128)(2,1)}, bf16[2,16,768]{2,1,0:T(8,128)(2,1)}) async-done(((bf16[2,16,768]{2,1,0:T(8,128)(2,1)}, bf16[2,16,768]{2,1,0:T(8,128)(2,1)}, bf16[2,16,768]{2,1,0:T(8,128)(2,1)}), (bf16[2,16,768]{2,1,0:T(8,128)(2,1)}, bf16[2,16,768]{2,1,0:T(8,128)(2,1)}, bf16[2,16,768]{2,1,0:T(8,128)(2,1)})) %all-reduce.6.cloned.1.call-update) | async-done | bytes 147472 | tf_op jit(solution)/shard_map/psum | solution.py:134
  263.8 4.0 convolution_convert_fusion.1
  267.9 3.2 convolution_convert_fusion
  271.1 0.2 reduce-scatter.4.cloned.1.call-start
  271.4 3.2 convolution_convert_fusion.2
  274.8 26.7 %all-reduce.8.cloned.1.call-done = (bf16[128,768]{1,0:T(8,128)(2,1)}, bf16[128,768]{1,0:T(8,128)(2,1)}, bf16[128,768]{1,0:T(8,128)(2,1)}) async-done(((bf16[128,768]{1,0:T(8,128)(2,1)}, bf16[128,768]{1,0:T(8,128)(2,1)}, bf16[128,768]{1,0:T(8,128)(2,1)}), (bf16[128,768]{1,0:T(8,128)(2,1)}, bf16[128,768]{1,0:T(8,128)(2,1)}, bf16[128,768]{1,0:T(8,128)(2,1)})) %all-reduce.8.cloned.1.call-update) | async-done | bytes 589840 | tf_op jit(solution)/shard_map/psum | solution.py:98
  301.5 1.6 fusion.10
  303.3 2.0 fusion.2
  305.3 2.9 fusion.1
  308.2 2.0 fusion
  310.2 0.7 fusion.22
  311.0 6.4 %all-reduce = (f32[8,1,16]{2,0,1:T(8,128)}, f32[32]{0:T(128)S(1)}) all-reduce(f32[8,1,16]{2,0,1:T(8,128)S(1)} %all_to_all.22, f32[32]{0:T(128)S(1)} %reshape.191), channel_id=1, replica_groups=mesh['grp'=4,'ep'=8] {'grp'}, use_global_device_ids=true, to_apply=%region_22.23 | all-reduce | flops 160 | bytes 1280 | tf_op jit(solution)/shard_map/psum | solution.py:163
  317.4 5.8 %all-to-all-start.3 = ((f32[8,1,16]{2,1,0:T(1,128)}), f32[8,1,16]{2,1,0:T(1,128)S(1)}, u32[]{:S(2)}, u32[]{:S(2)}) async-start(f32[8,1,16]{2,1,0:T(1,128)} %bitcast.19), calls=%async_computation.6 | async-start | bytes 8192 | tf_op jit(solution)/shard_map/all_to_all | solution.py:164
  323.3 0.2 convolution_reduce_fusion
  323.5 6.4 %all-to-all-done.3 = f32[8,1,16]{2,1,0:T(1,128)S(1)} async-done(((f32[8,1,16]{2,1,0:T(1,128)}), f32[8,1,16]{2,1,0:T(1,128)S(1)}, u32[]{:S(2)}, u32[]{:S(2)}) %all-to-all-start.3) | async-done | bytes 544 | tf_op jit(solution)/shard_map/all_to_all | solution.py:164
  329.9 0.5 broadcast.154
  330.4 0.7 reduce.11
  331.1 0.4 convolution_reduce_fusion.1
  331.7 0.7 copy.39
  332.4 57.6 %reduce-scatter.6.cloned.1.call-done = bf16[2,1280,96]{1,2,0:T(8,128)(2,1)} async-done(((bf16[2,1280,768]{1,2,0:T(8,128)(2,1)}), bf16[2,1280,96]{1,2,0:T(8,128)(2,1)}) %reduce-scatter.6.cloned.1.call-update) | async-done | bytes 491536 | tf_op jit(solution)/shard_map/reduce_scatter | solution.py:155
  390.0 2.0 convert_element_type.245
  392.0 85.7 %reduce-scatter.8.cloned.1.call-done = bf16[2,1280,96]{1,2,0:T(8,128)(2,1)} async-done(((bf16[2,1280,768]{1,2,0:T(8,128)(2,1)}), bf16[2,1280,96]{1,2,0:T(8,128)(2,1)}) %reduce-scatter.8.cloned.1.call-update) | async-done | bytes 491536 | tf_op jit(solution)/shard_map/reduce_scatter | solution.py:158
  477.7 2.0 convert_bitcast_fusion
  479.7 86.1 %reduce-scatter.4.cloned.1.call-done = bf16[2,1280,96]{1,2,0:T(8,128)(2,1)} async-done(((bf16[2,1280,768]{1,2,0:T(8,128)(2,1)}), bf16[2,1280,96]{1,2,0:T(8,128)(2,1)}) %reduce-scatter.4.cloned.1.call-update) | async-done | bytes 491536 | tf_op jit(solution)/shard_map/reduce_scatter | solution.py:152
  565.9 2.0 convert_element_type.242
  (59 shorter events, 2.5 us)
Async XLA Ops:
  7.2 227.2 %copy-start = (bf16[1,768,1280]{2,1,0:T(8,128)(2,1)S(1)}, bf16[1,768,1280]{2,1,0:T(8,128)(2,1)}, u32[]{:S(2)}) copy-start(bf16[1,768,1280]{2,1,0:T(8,128)(2,1)} %param.18) | copy-start | bytes 5898244
  7.2 24.8 %copy-start.2 = (bf16[256,1280]{1,0:T(8,128)(2,1)S(1)}, bf16[256,1280]{1,0:T(8,128)(2,1)}, u32[]{:S(2)}) copy-start(bf16[256,1280]{1,0:T(8,128)(2,1)} %param.11) | copy-start | bytes 1966084
  7.2 26.1 %copy-start.3 = (bf16[256,1280]{1,0:T(8,128)(2,1)S(1)}, bf16[256,1280]{1,0:T(8,128)(2,1)}, u32[]{:S(2)}) copy-start(bf16[256,1280]{1,0:T(8,128)(2,1)} %param.12) | copy-start | bytes 1966084
  7.2 81.2 %all-gather.8.cloned.1.call-start = ((), (), s32[]{:S(2)}) async-start(), calls=%async_computation.9 | async-start | bytes 4423680 | tf_op jit(solution)/shard_map/all_gather | solution.py:118
  7.9 151.8 %all-gather.6.cloned.1.call-start = ((), (), s32[]{:S(2)}) async-start(), calls=%async_computation.8 | async-start | bytes 4423680 | tf_op jit(solution)/shard_map/all_gather | solution.py:119
  8.7 221.7 %all-gather.4.cloned.1.call-start = ((), (), s32[]{:S(2)}) async-start(), calls=%async_computation.7 | async-start | bytes 4423680 | tf_op jit(solution)/shard_map/all_gather | solution.py:121
  17.9 15.6 %all-to-all-start.1 = ((bf16[8,1,16]{2,1,0:T(2,128)(2,1)}), bf16[8,1,16]{2,1,0:T(2,128)(2,1)S(1)}, u32[]{:S(2)}, u32[]{:S(2)}) async-start(bf16[8,1,16]{2,1,0:T(2,128)(2,1)} %all_to_all.24), calls=%async_computation.1 | async-start | bytes 8192 | tf_op jit(solution)/shard_map/all_to_all | solution.py:81
  33.5 18.3 %all-to-all-start = ((bf16[8,16,1280]{2,1,0:T(8,128)(2,1)}), bf16[8,16,1280]{2,1,0:T(8,128)(2,1)S(1)}, u32[]{:S(2)}, u32[]{:S(2)}) async-start(bf16[8,16,1280]{2,1,0:T(8,128)(2,1)} %bitcast.121), calls=%async_computation | async-start | bytes 655360 | tf_op jit(solution)/shard_map/all_to_all | solution.py:79
  51.8 23.6 %all-to-all-start.2 = ((bf16[8,16,1280]{2,1,0:T(8,128)(2,1)}), bf16[8,16,1280]{2,1,0:T(8,128)(2,1)S(1)}, u32[]{:S(2)}, u32[]{:S(2)}) async-start(bf16[8,16,1280]{2,1,0:T(8,128)(2,1)} %bitcast.122), calls=%async_computation.2 | async-start | bytes 655360 | tf_op jit(solution)/shard_map/all_to_all | solution.py:80
  56.7 207.0 %all-reduce.6.cloned.1.call-start = ((), (), s32[]{:S(2)}) async-start(), calls=%async_computation.13 | async-start | bytes 294912 | tf_op jit(solution)/shard_map/psum | solution.py:134
  234.3 67.2 %all-reduce.8.cloned.1.call-start = ((), (), s32[]{:S(2)}) async-start(), calls=%async_computation.14 | async-start | bytes 1179648 | tf_op jit(solution)/shard_map/psum | solution.py:98
  235.9 154.1 %reduce-scatter.6.cloned.1.call-start = ((), (), s32[]{:S(2)}) async-start(), calls=%async_computation.11 | async-start | bytes 4423680 | tf_op jit(solution)/shard_map/reduce_scatter | solution.py:155
  263.7 4.1 copy-start.5
  263.7 4.1 copy-start.6
  267.8 209.9 %reduce-scatter.8.cloned.1.call-start = ((), (), s32[]{:S(2)}) async-start(), calls=%async_computation.12 | async-start | bytes 4423680 | tf_op jit(solution)/shard_map/reduce_scatter | solution.py:158
  267.9 3.5 copy-start.9
  271.1 294.7 %reduce-scatter.4.cloned.1.call-start = ((), (), s32[]{:S(2)}) async-start(), calls=%async_computation.10 | async-start | bytes 4423680 | tf_op jit(solution)/shard_map/reduce_scatter | solution.py:152
  301.5 1.7 copy-start.4
  301.5 1.7 copy-start.7
  303.2 5.0 copy-start.8
  303.3 7.0 %copy-start.1 = (bf16[2,768,1280]{2,1,0:T(8,128)(2,1)S(1)}, bf16[2,768,1280]{2,1,0:T(8,128)(2,1)}, u32[]{:S(2)}) copy-start(bf16[2,768,1280]{2,1,0:T(8,128)(2,1)} %all-gather.4.cloned.1.call-done) | copy-start | bytes 11796484
  317.4 12.4 %all-to-all-start.3 = ((f32[8,1,16]{2,1,0:T(1,128)}), f32[8,1,16]{2,1,0:T(1,128)S(1)}, u32[]{:S(2)}, u32[]{:S(2)}) async-start(f32[8,1,16]{2,1,0:T(1,128)} %bitcast.19), calls=%async_computation.6 | async-start | bytes 8192 | tf_op jit(solution)/shard_map/all_to_all | solution.py:164
Sparse Core Ops, SparseCore 0:
  10.2 78.1 all-gather.7
  90.6 69.1 all-gather.5
  161.9 68.4 all-gather.3
  234.4 29.2 all-reduce.5
  266.9 34.6 all-reduce.7
  305.5 84.4 reduce-scatter.5
  393.7 83.9 reduce-scatter.7
  481.8 83.9 reduce-scatter.3
where the time goes:
time: 576 us; the launch traced here: 575 us
  waiting for transfers between devices  464 us (81%)
  matrix products  41.6 us (7%)
  starting transfers between devices  24.6 us (4%)
  between operations  14.4 us (2%)
  other arithmetic  12.2 us (2%)
  local copies, waits for them, and re-layouts  11.6 us (2%)
  blocking collectives  6.41 us (1%)
    reduce_scatter x1, waiting for transfers between devices, body(): lax.psum_scatter(shadow_gate.astype(jnp.bfloat16), 'ep', scatter_dimensio...  86.1 us
    reduce_scatter x1, waiting for transfers between devices, body(): lax.psum_scatter(shadow_down.astype(jnp.bfloat16), 'ep', scatter_dimensio...  85.7 us
    all_gather x1, waiting for transfers between devices, body(): lax.all_gather(up_hot, 'ep', axis=2, tiled=True)  67.5 us
    all_gather x1, waiting for transfers between devices, body(): full_down = lax.all_gather(down_hot, 'ep', axis=1, tiled=True)  66.8 us
    reduce_scatter x1, waiting for transfers between devices, body(): lax.psum_scatter(shadow_up.astype(jnp.bfloat16), 'ep', scatter_dimension=...  57.6 us
    psum x1, waiting for transfers between devices, body(): lax.psum(part_up_hot.astype(jnp.bfloat16), 'grp').astype(jnp.float32)  27.8 us
    psum x1, waiting for transfers between devices, body(): lax.psum(part_up.astype(jnp.bfloat16), 'grp').astype(jnp.float32)  26.7 us
    all_to_all x1, waiting for transfers between devices, body(): lax.all_to_all(outgoing[1], 'ep', split_axis=0, concat_axis=0, tiled=True)  13.3 us
  transfers between devices with their start and end apart: 12, of which 11 were waited for; matrix products, arithmetic and copies ran while one was open for 10% of the time, Pallas kernels for 0%

commit v1 on v0

--- a/solution.py
+++ b/solution.py
@@ -2,6 +2,36 @@
 import jax.numpy as jnp
 from jax import lax
 from jax.sharding import PartitionSpec as P
+
+
+def points_save(inp, join_dim):
+    x_new = list(inp.shape[1:])
+    x_new[join_dim] *= inp.shape[0]
+    next_value = jnp.moveaxis(inp, 0, join_dim).reshape(x_new)
+    return next_value
+
+
+def _try_all_skins(xin, ax_name, d_out):
+    wide_n = jax.lax.axis_size(ax_name)
+    log = [(dd, (dd + 1) % wide_n) for dd in range(wide_n)]
+    queue = [(at, ii) for ii, at in log]
+    t = 0
+    tall, finding = ([], [])
+    while t < wide_n - 1:
+        if t % 2 == 0:
+            u1 = jax.lax.ppermute(tall[-1] if tall else xin, ax_name, perm=log)
+            tall.append(u1)
+        else:
+            carry = jax.lax.ppermute(finding[-1] if finding else xin, ax_name, perm=queue)
+            finding.append(carry)
+        t += 1
+    odd = jnp.stack([*tall[::-1], xin, *finding])
+    v_next = jax.lax.axis_index(ax_name)
+    v_now = len(tall)
+    piece_now = v_next - v_now
+    odd = odd[(jnp.arange(wide_n) - piece_now) % wide_n]
+    e_now = points_save(odd, d_out)
+    return e_now
 
 
 def route_table(flat_ids, targets, capacity):
@@ -118,7 +148,7 @@
         lax.all_gather(gate_hot, "ep", axis=2, tiled=True),
         lax.all_gather(up_hot, "ep", axis=2, tiled=True),
     )
-    full_down = lax.all_gather(down_hot, "ep", axis=1, tiled=True)
+    full_down = _try_all_skins(down_hot, "ep", 1)
     hot_weighted = (
         hot_scale.astype(jnp.float32)[:, :, None] * hot_cotan.astype(jnp.float32)
     ).astype(jnp.bfloat16)

time: 576 us -> 557 us (0.967)
  waiting for transfers between devices: 464 us -> 403 us
  starting transfers between devices: 24.6 us -> 48.3 us
  local copies, waits for them, and re-layouts: 11.6 us -> 29.1 us
    all_gather x1 -> x0, waiting for transfers between devices: 66.8 us -> none  [body(): full_down = lax.all_gather(down_hot, 'ep', axis=1, tiled=True)]
    ppermute x0 -> x7, waiting for transfers between devices: none -> 50.9 us  [the longest x4 50.9 us: _try_all_skins(): u1 = jax.lax.ppermute(tall[-1] if tall else xin, ax_name, perm=log)]
    ppermute x0 -> x7, starting transfers between devices: none -> 26.5 us  [the longest x3 18.6 us: _try_all_skins(): jax.lax.ppermute(finding[-1] if finding else xin, ax_name, perm=queue)]
    unnamed x23 -> x46, local copies, waits for them, and re-layouts: 3.04 us -> 17.5 us
    all_gather x1, waiting for transfers between devices: 12.9 us -> 0.01 us  [body(): lax.all_gather(gate_hot, 'ep', axis=2, tiled=True)]
    all_to_all x1, waiting for transfers between devices: 13.3 us -> 0.49 us  [body(): lax.all_to_all(outgoing[1], 'ep', split_axis=0, concat_axis=0, tiled=True)]
    all_gather x1, waiting for transfers between devices: 67.5 us -> 57.9 us  [body(): lax.all_gather(up_hot, 'ep', axis=2, tiled=True)]
    all_to_all x1, waiting for transfers between devices: 11 us -> 1.64 us  [body(): lax.all_to_all(outgoing[0], 'ep', split_axis=0, concat_axis=0, tiled=True)]
  transfers between devices with their start and end apart: 12 -> 18, of which waited for: 11 -> 13; matrix products, arithmetic and copies ran while one was open for 10% -> 13% of each run, Pallas kernels for 0% -> 0%
where the time goes in v1:
time: 557 us; the launch traced here: 555 us
  waiting for transfers between devices  403 us (72%)
  starting transfers between devices  48.3 us (9%)
  matrix products  41.6 us (7%)
  local copies, waits for them, and re-layouts  29.1 us (5%)
  between operations  14.5 us (3%)
  other arithmetic  12.2 us (2%)
  blocking collectives  6.41 us (1%)
    reduce_scatter x1, waiting for transfers between devices, body(): lax.psum_scatter(shadow_gate.astype(jnp.bfloat16), 'ep', scatter_dimensio...  86.1 us
    reduce_scatter x1, waiting for transfers between devices, body(): lax.psum_scatter(shadow_down.astype(jnp.bfloat16), 'ep', scatter_dimensio...  85.5 us
    reduce_scatter x1, waiting for transfers between devices, body(): lax.psum_scatter(shadow_up.astype(jnp.bfloat16), 'ep', scatter_dimension=...  58.2 us
    all_gather x1, waiting for transfers between devices, body(): lax.all_gather(up_hot, 'ep', axis=2, tiled=True)  57.9 us
    ppermute x4, waiting for transfers between devices, _try_all_skins(): u1 = jax.lax.ppermute(tall[-1] if tall else xin, ax_name, perm=log)  50.9 us
    psum x1, waiting for transfers between devices, body(): lax.psum(part_up_hot.astype(jnp.bfloat16), 'grp').astype(jnp.float32)  27.8 us
    psum x1, waiting for transfers between devices, body(): lax.psum(part_up.astype(jnp.bfloat16), 'grp').astype(jnp.float32)  26.9 us
    ppermute x3, starting transfers between devices, _try_all_skins(): jax.lax.ppermute(finding[-1] if finding else xin, ax_name, perm=queue)  18.6 us
  transfers between devices with their start and end apart: 18, of which 13 were waited for; matrix products, arithmetic and copies ran while one was open for 13% of the time, Pallas kernels for 0%

profile of v1, /device:TPU:0, one launch (start us, length us, event | category | flops | bytes accessed | tf_op | source)
XLA Modules:
  0.0 555.4 jit_solution(9865971593276026440)
XLA Ops:
  7.2 0.7 all-gather.5.cloned.1.call-update
  7.9 3.0 collective-permute-start
  10.9 3.1 collective-permute-start.4
  14.1 0.8 copy.35
  15.2 0.8 copy.39
  16.2 2.3 reduce-window.14
  19.4 0.7 all_to_all.24
  20.1 3.3 all-to-all-start.1
  23.4 0.7 all-gather.3.cloned.1.call-update
  24.1 0.7 compare_convert_fusion.1
  25.9 0.8 fusion.77
  27.3 1.3 convolution_convert_fusion.8
  29.5 1.0 convolution_convert_fusion.7
  30.5 7.1 %collective-permute-done = bf16[2,96,1280]{2,1,0:T(8,128)(2,1)} collective-permute-done((bf16[2,96,1280]{2,1,0:T(8,128)(2,1)}, bf16[2,96,1280]{2,1,0:T(8,128)(2,1)}, u32[]{:S(2)}, u32[]{:S(2)}) %collective-permute-start) | collective-permute-done | bytes 491552 | tf_op jit(solution)/shard_map/ppermute | solution.py:22
  37.6 2.5 collective-permute-start.1
  40.3 4.9 all-to-all-start
  45.2 2.1 convolution_convert_fusion.6
  47.3 12.7 %collective-permute-done.1 = bf16[2,96,1280]{2,1,0:T(8,128)(2,1)} collective-permute-done((bf16[2,96,1280]{2,1,0:T(8,128)(2,1)}, bf16[2,96,1280]{2,1,0:T(8,128)(2,1)}, u32[]{:S(2)}, u32[]{:S(2)}) %collective-permute-start.1) | collective-permute-done | bytes 491552 | tf_op jit(solution)/shard_map/ppermute | solution.py:22
  60.0 4.7 collective-permute-start.5
  64.7 1.6 all-to-all-done
  66.3 7.2 %all-to-all-start.2 = ((bf16[8,16,1280]{2,1,0:T(8,128)(2,1)}), bf16[8,16,1280]{2,1,0:T(8,128)(2,1)S(1)}, u32[]{:S(2)}, u32[]{:S(2)}) async-start(bf16[8,16,1280]{2,1,0:T(8,128)(2,1)} %bitcast.5), calls=%async_computation.2 | async-start | bytes 655360 | tf_op jit(solution)/shard_map/all_to_all | solution.py:110
  73.6 2.7 fusion.16
  76.3 18.6 %collective-permute-done.2 = bf16[2,96,1280]{2,1,0:T(8,128)(2,1)} collective-permute-done((bf16[2,96,1280]{2,1,0:T(8,128)(2,1)}, bf16[2,96,1280]{2,1,0:T(8,128)(2,1)}, u32[]{:S(2)}, u32[]{:S(2)}) %collective-permute-start.2) | collective-permute-done | bytes 491552 | tf_op jit(solution)/shard_map/ppermute | solution.py:22
  94.9 2.5 collective-permute-start.3
  97.4 2.7 fusion.19
  100.7 10.7 %collective-permute-start.6 = (bf16[2,96,1280]{2,1,0:T(8,128)(2,1)}, bf16[2,96,1280]{2,1,0:T(8,128)(2,1)S(1)}, u32[]{:S(2)}, u32[]{:S(2)}) collective-permute-start(bf16[2,96,1280]{2,1,0:T(8,128)(2,1)} %collective-permute-done.5), channel_id=1, source_target_pairs={{1,0},{2,1},{3,2},{4,3},{5,4},{6,5},{7,6},{0,7},{9,8},{10,9},{11,1... | collective-permute-start | bytes 1474568 | tf_op jit(solution)/shard_map/ppermute | solution.py:25
  111.4 12.5 %collective-permute-done.3 = bf16[2,96,1280]{2,1,0:T(8,128)(2,1)} collective-permute-done((bf16[2,96,1280]{2,1,0:T(8,128)(2,1)}, bf16[2,96,1280]{2,1,0:T(8,128)(2,1)}, u32[]{:S(2)}, u32[]{:S(2)}) %collective-permute-start.3) | collective-permute-done | bytes 491552 | tf_op jit(solution)/shard_map/ppermute | solution.py:22
  123.9 1.9 bitcast_dynamic-update-slice_fusion.7
  125.8 1.9 bitcast_dynamic-update-slice_fusion.6
  127.7 1.9 bitcast_dynamic-update-slice_fusion.5
  129.6 1.8 bitcast_dynamic-update-slice_fusion.4
  131.4 1.8 bitcast_dynamic-update-slice_fusion.3
  133.3 1.9 bitcast_dynamic-update-slice_fusion.2
  135.2 1.9 bitcast_dynamic-update-slice_fusion.1
  137.0 0.8 bitcast_dynamic-update-slice_fusion
  137.8 4.9 gather_fusion
  142.7 2.4 copy.44
  145.1 2.0 copy-done.1
  147.0 1.8 convolution_convert_fusion.12
  148.8 4.0 convolution_convert_fusion.10
  152.8 57.9 %all-gather.3.cloned.1.call-done = bf16[2,1280,768]{1,2,0:T(8,128)(2,1)} async-done(((bf16[2,1280,96]{1,2,0:T(8,128)(2,1)}), bf16[2,1280,768]{1,2,0:T(8,128)(2,1)}) %all-gather.3.cloned.1.call-update) | async-done | bytes 3932176 | tf_op jit(solution)/shard_map/all_gather | solution.py:149
  210.7 3.9 convolution_convert_fusion.11
  214.6 1.5 fusion.13
  216.1 27.8 %all-reduce.6.cloned.1.call-done = (bf16[2,16,768]{2,1,0:T(8,128)(2,1)}, bf16[2,16,768]{2,1,0:T(8,128)(2,1)}, bf16[2,16,768]{2,1,0:T(8,128)(2,1)}) async-done(((bf16[2,16,768]{2,1,0:T(8,128)(2,1)}, bf16[2,16,768]{2,1,0:T(8,128)(2,1)}, bf16[2,16,768]{2,1,0:T(8,128)(2,1)}), (bf16[2,16,768]{2,1,0:T(8,128)(2,1)}, bf16[2,16,768]{2,1,0:T(8,128)(2,1)}, bf16[2,16,768]{2,1,0:T(8,128)(2,1)})) %all-reduce.6.cloned.1.call-update) | async-done | bytes 147472 | tf_op jit(solution)/shard_map/psum | solution.py:164
  244.0 4.0 convolution_convert_fusion.1
  248.1 3.1 convolution_convert_fusion
  251.5 3.2 convolution_convert_fusion.2
  254.9 26.9 %all-reduce.8.cloned.1.call-done = (bf16[128,768]{1,0:T(8,128)(2,1)}, bf16[128,768]{1,0:T(8,128)(2,1)}, bf16[128,768]{1,0:T(8,128)(2,1)}) async-done(((bf16[128,768]{1,0:T(8,128)(2,1)}, bf16[128,768]{1,0:T(8,128)(2,1)}, bf16[128,768]{1,0:T(8,128)(2,1)}), (bf16[128,768]{1,0:T(8,128)(2,1)}, bf16[128,768]{1,0:T(8,128)(2,1)}, bf16[128,768]{1,0:T(8,128)(2,1)})) %all-reduce.8.cloned.1.call-update) | async-done | bytes 589840 | tf_op jit(solution)/shard_map/psum | solution.py:128
  281.8 1.6 fusion.10
  283.5 2.0 fusion.2
  285.5 2.9 fusion.1
  288.5 2.0 fusion
  290.5 0.7 fusion.22
  291.3 6.4 %all-reduce = (f32[8,1,16]{2,0,1:T(8,128)}, f32[32]{0:T(128)S(1)}) all-reduce(f32[8,1,16]{2,0,1:T(8,128)S(1)} %all_to_all.22, f32[32]{0:T(128)S(1)} %reshape.244), channel_id=1, replica_groups=mesh['grp'=4,'ep'=8] {'grp'}, use_global_device_ids=true, to_apply=%region_22.23 | all-reduce | flops 160 | bytes 1280 | tf_op jit(solution)/shard_map/psum | solution.py:193
  297.7 5.8 %all-to-all-start.3 = ((f32[8,1,16]{2,1,0:T(1,128)}), f32[8,1,16]{2,1,0:T(1,128)S(1)}, u32[]{:S(2)}, u32[]{:S(2)}) async-start(f32[8,1,16]{2,1,0:T(1,128)} %bitcast.30), calls=%async_computation.6 | async-start | bytes 8192 | tf_op jit(solution)/shard_map/all_to_all | solution.py:194
  303.8 6.4 %all-to-all-done.3 = f32[8,1,16]{2,1,0:T(1,128)S(1)} async-done(((f32[8,1,16]{2,1,0:T(1,128)}), f32[8,1,16]{2,1,0:T(1,128)S(1)}, u32[]{:S(2)}, u32[]{:S(2)}) %all-to-all-start.3) | async-done | bytes 544 | tf_op jit(solution)/shard_map/all_to_all | solution.py:194
  310.7 0.7 reduce.11
  312.0 0.7 copy.46
  312.6 58.2 %reduce-scatter.6.cloned.1.call-done = bf16[2,1280,96]{1,2,0:T(8,128)(2,1)} async-done(((bf16[2,1280,768]{1,2,0:T(8,128)(2,1)}), bf16[2,1280,96]{1,2,0:T(8,128)(2,1)}) %reduce-scatter.6.cloned.1.call-update) | async-done | bytes 491536 | tf_op jit(solution)/shard_map/reduce_scatter | solution.py:185
  370.8 2.0 convert_element_type.245
  372.9 85.5 %reduce-scatter.8.cloned.1.call-done = bf16[2,1280,96]{1,2,0:T(8,128)(2,1)} async-done(((bf16[2,1280,768]{1,2,0:T(8,128)(2,1)}), bf16[2,1280,96]{1,2,0:T(8,128)(2,1)}) %reduce-scatter.8.cloned.1.call-update) | async-done | bytes 491536 | tf_op jit(solution)/shard_map/reduce_scatter | solution.py:188
  458.4 2.0 convert_bitcast_fusion
  460.4 86.1 %reduce-scatter.4.cloned.1.call-done = bf16[2,1280,96]{1,2,0:T(8,128)(2,1)} async-done(((bf16[2,1280,768]{1,2,0:T(8,128)(2,1)}), bf16[2,1280,96]{1,2,0:T(8,128)(2,1)}) %reduce-scatter.4.cloned.1.call-update) | async-done | bytes 491536 | tf_op jit(solution)/shard_map/reduce_scatter | solution.py:182
  546.5 2.0 convert_element_type.242
  (98 shorter events, 6.9 us)
Async XLA Ops:
  7.2 207.4 %copy-start = (bf16[1,768,1280]{2,1,0:T(8,128)(2,1)S(1)}, bf16[1,768,1280]{2,1,0:T(8,128)(2,1)}, u32[]{:S(2)}) copy-start(bf16[1,768,1280]{2,1,0:T(8,128)(2,1)} %param.18) | copy-start | bytes 5898244
  7.2 21.4 %copy-start.3 = (bf16[256,1280]{1,0:T(8,128)(2,1)S(1)}, bf16[256,1280]{1,0:T(8,128)(2,1)}, u32[]{:S(2)}) copy-start(bf16[256,1280]{1,0:T(8,128)(2,1)} %param.11) | copy-start | bytes 1966084
  7.2 141.6 %all-gather.5.cloned.1.call-start = ((), (), s32[]{:S(2)}) async-start(), calls=%async_computation.8 | async-start | bytes 4423680 | tf_op jit(solution)/shard_map/all_gather | solution.py:148
  7.9 29.7 %collective-permute-start = (bf16[2,96,1280]{2,1,0:T(8,128)(2,1)}, bf16[2,96,1280]{2,1,0:T(8,128)(2,1)}, u32[]{:S(2)}, u32[]{:S(2)}) collective-permute-start(bf16[2,96,1280]{2,1,0:T(8,128)(2,1)} %param.21), channel_id=1, source_target_pairs={{0,1},{1,2},{2,3},{3,4},{4,5},{5,6},{6,7},{7,0},{8,9},{9,10},{10,1... | collective-permute-start | bytes 1474568 | tf_op jit(solution)/shard_map/ppermute | solution.py:22
  10.9 49.0 %collective-permute-start.4 = (bf16[2,96,1280]{2,1,0:T(8,128)(2,1)}, bf16[2,96,1280]{2,1,0:T(8,128)(2,1)}, u32[]{:S(2)}, u32[]{:S(2)}) collective-permute-start(bf16[2,96,1280]{2,1,0:T(8,128)(2,1)} %param.21), channel_id=1, source_target_pairs={{1,0},{2,1},{3,2},{4,3},{5,4},{6,5},{7,6},{0,7},{9,8},{10,9},{11,1... | collective-permute-start | bytes 1474568 | tf_op jit(solution)/shard_map/ppermute | solution.py:25
  19.1 10.2 %copy-start.14 = (pred[1536]{0:T(1024)(128)(4,1)}, pred[1536]{0:T(1024)(128)(4,1)S(1)}, u32[]{:S(2)}) copy-start(pred[1536]{0:T(1024)(128)(4,1)S(1)} %broadcast_compare_fusion.1) | copy-start | bytes 4612
  19.1 9.7 %copy-start.10 = (s32[1536]{0:T(1024)}, s32[1536]{0:T(1024)S(1)}, u32[]{:S(2)}) copy-start(s32[1536]{0:T(1024)S(1)} %multiply_add_fusion.1) | copy-start | bytes 18436
  20.1 20.2 %all-to-all-start.1 = ((bf16[8,1,16]{2,1,0:T(2,128)(2,1)}), bf16[8,1,16]{2,1,0:T(2,128)(2,1)S(1)}, u32[]{:S(2)}, u32[]{:S(2)}) async-start(bf16[8,1,16]{2,1,0:T(2,128)(2,1)} %all_to_all.24), calls=%async_computation.1 | async-start | bytes 8192 | tf_op jit(solution)/shard_map/all_to_all | solution.py:111
  23.4 187.3 %all-gather.3.cloned.1.call-start = ((), (), s32[]{:S(2)}) async-start(), calls=%async_computation.7 | async-start | bytes 4423680 | tf_op jit(solution)/shard_map/all_gather | solution.py:149
  26.7 13.6 %copy-start.12 = (s32[1536]{0:T(1024)}, s32[1536]{0:T(1024)S(1)}, u32[]{:S(2)}) copy-start(s32[1536]{0:T(1024)S(1)} %multiply_add_fusion) | copy-start | bytes 18436
  26.9 13.3 %copy-start.16 = (pred[1536]{0:T(1024)(128)(4,1)}, pred[1536]{0:T(1024)(128)(4,1)S(1)}, u32[]{:S(2)}) copy-start(pred[1536]{0:T(1024)(128)(4,1)S(1)} %broadcast_compare_fusion) | copy-start | bytes 4612
  37.6 22.4 %collective-permute-start.1 = (bf16[2,96,1280]{2,1,0:T(8,128)(2,1)}, bf16[2,96,1280]{2,1,0:T(8,128)(2,1)}, u32[]{:S(2)}, u32[]{:S(2)}) collective-permute-start(bf16[2,96,1280]{2,1,0:T(8,128)(2,1)} %collective-permute-done), channel_id=1, source_target_pairs={{0,1},{1,2},{2,3},{3,4},{4,5},{5,6},{6,7},{7,0},{8,9},{9,10},{10,1... | collective-permute-start | bytes 1474568 | tf_op jit(solution)/shard_map/ppermute | solution.py:22
  40.3 26.1 %all-to-all-start = ((bf16[8,16,1280]{2,1,0:T(8,128)(2,1)}), bf16[8,16,1280]{2,1,0:T(8,128)(2,1)S(1)}, u32[]{:S(2)}, u32[]{:S(2)}) async-start(bf16[8,16,1280]{2,1,0:T(8,128)(2,1)} %bitcast.1), calls=%async_computation | async-start | bytes 655360 | tf_op jit(solution)/shard_map/all_to_all | solution.py:109
  60.0 35.0 %collective-permute-start.2 = (bf16[2,96,1280]{2,1,0:T(8,128)(2,1)}, bf16[2,96,1280]{2,1,0:T(8,128)(2,1)}, u32[]{:S(2)}, u32[]{:S(2)}) collective-permute-start(bf16[2,96,1280]{2,1,0:T(8,128)(2,1)} %collective-permute-done.1), channel_id=1, source_target_pairs={{0,1},{1,2},{2,3},{3,4},{4,5},{5,6},{6,7},{7,0},{8,9},{9,10},{10,1... | collective-permute-start | bytes 1474568 | tf_op jit(solution)/shard_map/ppermute | solution.py:22
  60.0 40.7 %collective-permute-start.5 = (bf16[2,96,1280]{2,1,0:T(8,128)(2,1)}, bf16[2,96,1280]{2,1,0:T(8,128)(2,1)}, u32[]{:S(2)}, u32[]{:S(2)}) collective-permute-start(bf16[2,96,1280]{2,1,0:T(8,128)(2,1)} %collective-permute-done.4), channel_id=1, source_target_pairs={{1,0},{2,1},{3,2},{4,3},{5,4},{6,5},{7,6},{0,7},{9,8},{10,9},{11,1... | collective-permute-start | bytes 1474568 | tf_op jit(solution)/shard_map/ppermute | solution.py:25
  66.3 34.2 %all-to-all-start.2 = ((bf16[8,16,1280]{2,1,0:T(8,128)(2,1)}), bf16[8,16,1280]{2,1,0:T(8,128)(2,1)S(1)}, u32[]{:S(2)}, u32[]{:S(2)}) async-start(bf16[8,16,1280]{2,1,0:T(8,128)(2,1)} %bitcast.5), calls=%async_computation.2 | async-start | bytes 655360 | tf_op jit(solution)/shard_map/all_to_all | solution.py:110
  73.6 170.4 %all-reduce.6.cloned.1.call-start = ((), (), s32[]{:S(2)}) async-start(), calls=%async_computation.12 | async-start | bytes 294912 | tf_op jit(solution)/shard_map/psum | solution.py:164
  94.9 29.0 %collective-permute-start.3 = (bf16[2,96,1280]{2,1,0:T(8,128)(2,1)}, bf16[2,96,1280]{2,1,0:T(8,128)(2,1)}, u32[]{:S(2)}, u32[]{:S(2)}) collective-permute-start(bf16[2,96,1280]{2,1,0:T(8,128)(2,1)} %collective-permute-done.2), channel_id=1, source_target_pairs={{0,1},{1,2},{2,3},{3,4},{4,5},{5,6},{6,7},{7,0},{8,9},{9,10},{10,1... | collective-permute-start | bytes 1474568 | tf_op jit(solution)/shard_map/ppermute | solution.py:22
  100.7 36.3 %collective-permute-start.6 = (bf16[2,96,1280]{2,1,0:T(8,128)(2,1)}, bf16[2,96,1280]{2,1,0:T(8,128)(2,1)S(1)}, u32[]{:S(2)}, u32[]{:S(2)}) collective-permute-start(bf16[2,96,1280]{2,1,0:T(8,128)(2,1)} %collective-permute-done.5), channel_id=1, source_target_pairs={{1,0},{2,1},{3,2},{4,3},{5,4},{6,5},{7,6},{0,7},{9,8},{10,9},{11,1... | collective-permute-start | bytes 1474568 | tf_op jit(solution)/shard_map/ppermute | solution.py:25
  145.1 2.0 copy-start.1
  214.5 67.3 %all-reduce.8.cloned.1.call-start = ((), (), s32[]{:S(2)}) async-start(), calls=%async_computation.13 | async-start | bytes 1179648 | tf_op jit(solution)/shard_map/psum | solution.py:128
  216.1 154.7 %reduce-scatter.6.cloned.1.call-start = ((), (), s32[]{:S(2)}) async-start(), calls=%async_computation.10 | async-start | bytes 4423680 | tf_op jit(solution)/shard_map/reduce_scatter | solution.py:185
  244.0 4.1 copy-start.5
  244.0 4.1 copy-start.6
  248.0 210.4 %reduce-scatter.8.cloned.1.call-start = ((), (), s32[]{:S(2)}) async-start(), calls=%async_computation.11 | async-start | bytes 4423680 | tf_op jit(solution)/shard_map/reduce_scatter | solution.py:188
  248.1 3.4 copy-start.9
  251.2 295.3 %reduce-scatter.4.cloned.1.call-start = ((), (), s32[]{:S(2)}) async-start(), calls=%async_computation.9 | async-start | bytes 4423680 | tf_op jit(solution)/shard_map/reduce_scatter | solution.py:182
  281.8 1.7 copy-start.4
  281.8 1.7 copy-start.7
  283.4 5.0 copy-start.8
  283.5 7.0 %copy-start.2 = (bf16[2,8,96,1280]{3,2,1,0:T(8,128)(2,1)S(1)}, bf16[2,8,96,1280]{3,2,1,0:T(8,128)(2,1)}, u32[]{:S(2)}) copy-start(bf16[2,8,96,1280]{3,2,1,0:T(8,128)(2,1)} %copy-done.1) | copy-start | bytes 11796484
  288.5 15.1 %copy-start.13 = (s32[1536]{0:T(1024)S(1)}, s32[1536]{0:T(1024)}, u32[]{:S(2)}) copy-start(s32[1536]{0:T(1024)} %copy-done.12) | copy-start | bytes 18436
  288.5 15.1 %copy-start.17 = (pred[1536]{0:T(1024)(128)(4,1)S(1)}, pred[1536]{0:T(1024)(128)(4,1)}, u32[]{:S(2)}) copy-start(pred[1536]{0:T(1024)(128)(4,1)} %copy-done.16) | copy-start | bytes 4612
  288.5 22.9 %copy-start.11 = (s32[1536]{0:T(1024)S(1)}, s32[1536]{0:T(1024)}, u32[]{:S(2)}) copy-start(s32[1536]{0:T(1024)} %copy-done.10) | copy-start | bytes 18436
  288.5 22.9 %copy-start.15 = (pred[1536]{0:T(1024)(128)(4,1)S(1)}, pred[1536]{0:T(1024)(128)(4,1)}, u32[]{:S(2)}) copy-start(pred[1536]{0:T(1024)(128)(4,1)} %copy-done.14) | copy-start | bytes 4612
  297.7 12.4 %all-to-all-start.3 = ((f32[8,1,16]{2,1,0:T(1,128)}), f32[8,1,16]{2,1,0:T(1,128)S(1)}, u32[]{:S(2)}, u32[]{:S(2)}) async-start(f32[8,1,16]{2,1,0:T(1,128)} %bitcast.30), calls=%async_computation.6 | async-start | bytes 8192 | tf_op jit(solution)/shard_map/all_to_all | solution.py:194
Sparse Core Ops, SparseCore 0:
  10.2 128.9 all-gather.4
  141.4 69.2 all-gather.2
  214.7 29.2 all-reduce.5
  247.1 34.6 all-reduce.7
  285.8 84.9 reduce-scatter.5
  374.4 83.9 reduce-scatter.7
  462.5 83.9 reduce-scatter.3
